TPU v7x, 256 devices: a whole 4x4x8 slice. The times are simulated.
256 devices in a mesh: dp: 32 (over z, y), tensor: 8 (over x, core).
Axes of the slice: x: 4, y: 4, z: 8, core: 2. Of those that a mesh axis runs over, the one named last changes fastest.
Arguments:
- tokens: bfloat16 [4096, 4096], P('dp', 'tensor'), may hold values from -6 to 6
- grad_out: bfloat16 [4096, 4096], P('dp', 'tensor'), may hold values from -6 to 6
- gate_blocks: int32 [8, 32], P('tensor'), may hold values from -1 to 447, as said below
- gate_values: bfloat16 [8, 32, 128, 128], P('tensor'), may hold values from -0.375 to 0.375
- up_blocks: int32 [8, 32], P('tensor'), may hold values from -1 to 447, as said below
- up_values: bfloat16 [8, 32, 128, 128], P('tensor'), may hold values from -0.375 to 0.375
- down_blocks: int32 [8, 32], P('tensor'), may hold values from -1 to 447, as said below
- down_values: bfloat16 [8, 32, 128, 128], P('tensor'), may hold values from -0.1875 to 0.1875
Outputs:
- mixed: bfloat16 [4096, 4096], P('dp', 'tensor')
- grad_tokens: bfloat16 [4096, 4096], P('dp', 'tensor')
- grad_gate: float32 [8, 32, 128, 128], P('tensor', 'dp')
- grad_up: float32 [8, 32, 128, 128], P('tensor', 'dp')
- grad_down: float32 [8, 32, 128, 128], P('tensor', 'dp')
Inputs may be any that keep to these rules, and one draw needn't show every extreme that they name: `gate_blocks`: each row lists distinct block numbers of one tensor shard in its first slots and -1 in the rest; a row has 16 to 32 listed blocks, one row has exactly 32 and another exactly 16. `up_blocks`: as for gate_blocks, drawn apart. `down_blocks`: as for gate_blocks, drawn apart.
All inputs are finite; a program needn't handle non-finite values.
Results may differ from a plain program's by a relative error of at most 0.015.
Values may be sent and summed in bfloat16 or wider, within the bound.
No kernel may reach another device: no remote copies, remote signals or barrier semaphores. Data moves between devices by JAX's collectives and lax.ppermute only.
A program may use at most 64 MiB of HBM per device.

v0:
```python
import jax
import jax.numpy as jnp
from jax import lax
from jax.sharding import PartitionSpec as P

FF = 14336


def locate(blocks, feature_count):
    flat = blocks[0]
    weight = (flat >= 0).astype(jnp.float32)
    safe = jnp.maximum(flat, 0)
    return (safe // feature_count, safe % feature_count, weight)


def one_hot(targets, weight, count):
    return (targets[:, None] == jnp.arange(count)[None, :]).astype(jnp.float32) * weight[:, None]


def spread(product, table):
    return jnp.einsum("tsn,sc->tcn", product, table, precision=lax.Precision.HIGHEST)


def select(source, position):
    return jnp.take(source, position, axis=1)


def forward_blocks(rows_in, values):
    return jnp.einsum("tsk,skn->tsn", rows_in, values, preferred_element_type=jnp.float32)


def backward_blocks(rows_in, values):
    return jnp.einsum("tsn,skn->tsk", rows_in, values, preferred_element_type=jnp.float32)


def slot_term(left, right, weight):
    product = jnp.einsum("tsk,tsn->skn", left, right, preferred_element_type=jnp.float32)
    return product * weight[:, None, None]


def body(
    tokens, grad_out, gate_blocks, gate_values, up_blocks, up_values, down_blocks, down_values
):
    gathered_x, gathered_dy = (
        lax.all_gather(tokens, "tensor", axis=1, tiled=True),
        lax.all_gather(grad_out, "tensor", axis=1, tiled=True),
    )
    tok_rows, feature_width = gathered_x.shape
    block_size = gate_values.shape[-1]
    feature_count = feature_width // block_size
    hidden_count = FF // (block_size * lax.axis_size("tensor"))
    inputs = gathered_x.reshape(tok_rows, feature_count, block_size)
    upstream = gathered_dy.reshape(tok_rows, feature_count, block_size)
    gate_hid, gate_feat, gate_live = locate(gate_blocks, feature_count)
    up_hid, up_feat, up_live = locate(up_blocks, feature_count)
    down_hid, down_feat, down_live = locate(down_blocks, feature_count)
    gate_rows = select(inputs, gate_feat)
    up_rows = select(inputs, up_feat)
    gate_pre = spread(
        forward_blocks(gate_rows, gate_values[0]), one_hot(gate_hid, gate_live, hidden_count)
    )
    up_pre = spread(forward_blocks(up_rows, up_values[0]), one_hot(up_hid, up_live, hidden_count))
    sigma_gate = jax.nn.sigmoid(gate_pre)
    activated = gate_pre * sigma_gate
    hidden = (activated * up_pre).astype(jnp.bfloat16)
    hidden_rows = select(hidden, down_hid)
    mixed_part = spread(
        forward_blocks(hidden_rows, down_values[0]), one_hot(down_feat, down_live, feature_count)
    )
    mixed_part = mixed_part.reshape(tok_rows, feature_width)
    upstream_rows = select(upstream, down_feat)
    mixed = lax.psum_scatter(
        mixed_part.astype(jnp.bfloat16), "tensor", scatter_dimension=1, tiled=True
    )
    hidden_grad = spread(
        backward_blocks(upstream_rows, down_values[0]), one_hot(down_hid, down_live, hidden_count)
    )
    gate_delta = (hidden_grad * up_pre * sigma_gate * (1.0 + gate_pre * (1.0 - sigma_gate))).astype(
        jnp.bfloat16
    )
    up_delta = (hidden_grad * activated).astype(jnp.bfloat16)
    gate_delta_rows = select(gate_delta, gate_hid)
    up_delta_rows = select(up_delta, up_hid)
    input_part = spread(
        backward_blocks(gate_delta_rows, gate_values[0]),
        one_hot(gate_feat, gate_live, feature_count),
    )
    input_part = input_part + spread(
        backward_blocks(up_delta_rows, up_values[0]), one_hot(up_feat, up_live, feature_count)
    )
    input_part = input_part.reshape(tok_rows, feature_width)
    gate_term = slot_term(gate_rows, gate_delta_rows, gate_live)
    up_term = slot_term(up_rows, up_delta_rows, up_live)
    down_term = slot_term(hidden_rows, upstream_rows, down_live)
    combined = lax.psum_scatter(
        jnp.stack([gate_term, up_term, down_term], axis=1).astype(jnp.bfloat16),
        "dp",
        scatter_dimension=0,
        tiled=True,
    ).astype(jnp.float32)
    grad_gate = combined[None, :, 0]
    grad_up = combined[None, :, 1]
    grad_down = combined[None, :, 2]
    grad_tokens = lax.psum_scatter(
        input_part.astype(jnp.bfloat16), "tensor", scatter_dimension=1, tiled=True
    )
    return (mixed, grad_tokens, grad_gate, grad_up, grad_down)


def solution(mesh):
    in_specs = (
        P("dp", "tensor"),
        P("dp", "tensor"),
        P("tensor", None),
        P("tensor", None, None, None),
        P("tensor", None),
        P("tensor", None, None, None),
        P("tensor", None),
        P("tensor", None, None, None),
    )
    out_specs = (
        P("dp", "tensor"),
        P("dp", "tensor"),
        P("tensor", "dp", None, None),
        P("tensor", "dp", None, None),
        P("tensor", "dp", None, None),
    )
    return jax.shard_map(body, mesh=mesh, in_specs=in_specs, out_specs=out_specs, check_vma=False)
```

profile of v0, /device:TPU:8, one launch (start us, length us, event | category | flops | bytes accessed | tf_op | source)
XLA Modules:
  0.0 338.6 jit_solution(3957242304848105937)
XLA Ops:
  7.2 1.7 copy.68
  9.0 0.0 all-gather.5.cloned.1.call-start
  9.0 1.7 copy.76
  10.7 0.0 all-reduce.3.cloned.1.call-start
  10.8 0.7 compare_and_fusion.1
  11.5 0.7 compare_and_fusion
  12.2 0.7 compare_and_fusion.2
  13.0 0.7 fusion.81
  13.6 0.7 fusion.82
  14.3 0.7 fusion.80
  14.9 24.2 %all-gather.3.cloned.1.call-done = bf16[128,4096]{0,1:T(8,128)(2,1)} async-done(((bf16[128,512]{0,1:T(8,128)(2,1)}), bf16[128,4096]{0,1:T(8,128)(2,1)}) %all-gather.3.cloned.1.call-update) | async-done | bytes 1048592 | tf_op jit(solution)/shard_map/all_gather | solution.py:45
  39.1 1.6 copy.69
  40.7 1.7 gather_fusion
  42.4 1.7 gather_fusion.1
  44.0 23.2 %all-gather.5.cloned.1.call-done = bf16[128,4096]{0,1:T(8,128)(2,1)} async-done(((bf16[128,512]{0,1:T(8,128)(2,1)}), bf16[128,4096]{0,1:T(8,128)(2,1)}) %all-gather.5.cloned.1.call-update) | async-done | bytes 1048592 | tf_op jit(solution)/shard_map/all_gather | solution.py:46
  67.2 2.3 copy.77
  69.5 0.5 convolution_bitcast_fusion.5
  70.0 3.2 fusion.10
  73.2 0.5 convolution_bitcast_fusion.4
  73.8 3.3 fusion.8
  77.0 2.9 gather_fusion.3
  79.9 2.1 convolution_bitcast_fusion.2
  82.0 2.2 fusion.4
  84.3 1.1 fusion.40
  85.4 1.7 gather_fusion.4
  87.0 3.2 fusion.17
  90.2 1.7 gather_fusion.5
  91.9 3.2 fusion.18
  95.1 1.7 gather_fusion.2
  96.8 2.5 fusion.19
  99.4 2.0 pad_maximum_fusion
  101.5 0.0 reduce-scatter.8.cloned.1.call-start
  101.5 2.2 convolution_bitcast_fusion
  103.7 0.9 convolution_bitcast_fusion.1
  104.6 3.0 fusion
  107.6 3.1 add_convert_fusion
  110.8 1.4 copy.123
  112.2 0.3 reduce-scatter.6.cloned.1.call-start
  112.5 0.2 copy-done.4
  112.7 0.5 convolution_bitcast_fusion.3
  113.2 3.0 fusion.14
  116.2 1.5 copy.124
  117.8 0.6 dynamic-slice
  118.4 140.7 %all-reduce.3.cloned.1.call-done = bf16[32,3,128,128]{3,2,0,1:T(8,128)(2,1)} async-done(((bf16[32,3,128,128]{3,2,0,1:T(8,128)(2,1)}), bf16[32,3,128,128]{3,2,0,1:T(8,128)(2,1)}) %all-reduce.3.cloned.1.call-update) | async-done | bytes 3145744
  259.0 1.6 dynamic-slice_convert_fusion
  260.6 0.7 slice_bitcast_fusion
  261.3 34.3 %reduce-scatter.8.cloned.1.call-done = bf16[128,512]{1,0:T(8,128)(2,1)} async-done(((bf16[128,4096]{1,0:T(8,128)(2,1)}), bf16[128,512]{1,0:T(8,128)(2,1)}) %reduce-scatter.8.cloned.1.call-update) | async-done | bytes 131088 | tf_op jit(solution)/shard_map/reduce_scatter | solution.py:104
  295.5 36.6 %reduce-scatter.6.cloned.1.call-done = bf16[128,512]{1,0:T(8,128)(2,1)} async-done(((bf16[128,4096]{1,0:T(8,128)(2,1)}), bf16[128,512]{1,0:T(8,128)(2,1)}) %reduce-scatter.6.cloned.1.call-update) | async-done | bytes 131088 | tf_op jit(solution)/shard_map/reduce_scatter | solution.py:72
  (43 shorter events, 0.2 us)
Async XLA Ops:
  7.2 66.1 %copy-start = (bf16[1,32,128,128]{3,2,1,0:T(8,128)(2,1)S(1)}, bf16[1,32,128,128]{3,2,1,0:T(8,128)(2,1)}, u32[]{:S(2)}) copy-start(bf16[1,32,128,128]{3,2,1,0:T(8,128)(2,1)} %param.17) | copy-start | bytes 3145732
  7.2 31.9 %all-gather.3.cloned.1.call-start = ((), (), s32[]{:S(2)}) async-start(), calls=%async_computation.2 | async-start | bytes 1179648 | tf_op jit(solution)/shard_map/all_gather | solution.py:45
  9.0 58.3 %all-gather.5.cloned.1.call-start = ((), (), s32[]{:S(2)}) async-start(), calls=%async_computation.4 | async-start | bytes 1179648 | tf_op jit(solution)/shard_map/all_gather | solution.py:46
  10.7 248.3 %all-reduce.3.cloned.1.call-start = ((), (), s32[]{:S(2)}) async-start(), calls=%async_computation.6 | async-start | bytes 6291456
  42.4 27.1 %copy-start.1 = (bf16[1,32,128,128]{3,2,1,0:T(8,128)(2,1)S(1)}, bf16[1,32,128,128]{3,2,1,0:T(8,128)(2,1)}, u32[]{:S(2)}) copy-start(bf16[1,32,128,128]{3,2,1,0:T(8,128)(2,1)} %param.15) | copy-start | bytes 3145732
  44.0 25.5 %copy-start.7 = (bf16[32,128,128]{2,1,0:T(8,128)(2,1)S(1)}, bf16[32,128,128]{2,1,0:T(8,128)(2,1)}, u32[]{:S(2)}) copy-start(bf16[32,128,128]{2,1,0:T(8,128)(2,1)} %gather_fusion) | copy-start | bytes 3145732
  70.0 3.2 copy-start.5
  73.7 6.2 %copy-start.2 = (bf16[1,32,128,128]{3,2,1,0:T(8,128)(2,1)S(1)}, bf16[1,32,128,128]{3,2,1,0:T(8,128)(2,1)}, u32[]{:S(2)}) copy-start(bf16[1,32,128,128]{3,2,1,0:T(8,128)(2,1)} %param.19) | copy-start | bytes 3145732
  82.0 2.3 copy-start.8
  82.0 2.3 copy-start.9
  96.8 2.5 copy-start.10
  96.8 2.6 copy-start.11
  101.5 2.3 copy-start.6
  101.5 194.1 %reduce-scatter.8.cloned.1.call-start = ((), (), s32[]{:S(2)}) async-start(), calls=%async_computation.5 | async-start | bytes 1179648 | tf_op jit(solution)/shard_map/reduce_scatter | solution.py:104
  110.8 1.7 copy-start.3
  110.8 1.9 copy-start.4
  112.2 219.9 %reduce-scatter.6.cloned.1.call-start = ((), (), s32[]{:S(2)}) async-start(), calls=%async_computation.3 | async-start | bytes 1179648 | tf_op jit(solution)/shard_map/reduce_scatter | solution.py:72
  116.2 1.5 copy-start.12
Sparse Core Ops, SparseCore 0:
  10.4 28.6 all-gather.2
  41.5 25.6 all-gather.4
  101.6 157.3 all-reduce.2
  262.0 33.5 reduce-scatter.7
  298.5 33.5 reduce-scatter.5
where the time goes:
time: 339 us
  waiting for transfers between devices  259 us (76%)
  matrix products  33.4 us (10%)
  local copies, waits for them, and re-layouts  23 us (7%)
  between operations  14.1 us (4%)
  other arithmetic  8.69 us (3%)
    unnamed x6, waiting for transfers between devices  141 us
    reduce_scatter x1, waiting for transfers between devices, body(): lax.psum_scatter(mixed_part.astype(jnp.bfloat16), 'tensor', scatter_dimen...  36.6 us
    reduce_scatter x1, waiting for transfers between devices, body(): lax.psum_scatter(input_part.astype(jnp.bfloat16), 'tensor', scatter_dimen...  34.3 us
    all_gather x1, waiting for transfers between devices, body(): lax.all_gather(tokens, 'tensor', axis=1, tiled=True)  24.2 us
    all_gather x1, waiting for transfers between devices, body(): lax.all_gather(grad_out, 'tensor', axis=1, tiled=True)  23.2 us
    dot_general x6, matrix products, spread(): jnp.einsum('tsn,sc->tcn', product, table, precision=lax.Precision.HIGHEST)  17.9 us
    gather x6, local copies, waits for them, and re-layouts, select(): return jnp.take(source, position, axis=1)  11.3 us
    dot_general x3, matrix products, slot_term(): jnp.einsum('tsk,tsn->skn', left, right, preferred_element_type=jnp.float32)  8.89 us
  transfers between devices with their start and end apart: 5, of which 5 were waited for; matrix products, arithmetic and copies ran while one was open for 9% of the time, Pallas kernels for 0%

commit v1 on v0

--- a/solution.py
+++ b/solution.py
@@ -92,15 +92,11 @@
     gate_term = slot_term(gate_rows, gate_delta_rows, gate_live)
     up_term = slot_term(up_rows, up_delta_rows, up_live)
     down_term = slot_term(hidden_rows, upstream_rows, down_live)
-    combined = lax.psum_scatter(
-        jnp.stack([gate_term, up_term, down_term], axis=1).astype(jnp.bfloat16),
-        "dp",
-        scatter_dimension=0,
-        tiled=True,
-    ).astype(jnp.float32)
-    grad_gate = combined[None, :, 0]
-    grad_up = combined[None, :, 1]
-    grad_down = combined[None, :, 2]
+    grad_gate, grad_up, grad_down = (
+        lax.psum_scatter(term.astype(jnp.bfloat16), "dp", scatter_dimension=0, tiled=True)
+        .astype(jnp.float32)[None]
+        for term in (gate_term, up_term, down_term)
+    )
     grad_tokens = lax.psum_scatter(
         input_part.astype(jnp.bfloat16), "tensor", scatter_dimension=1, tiled=True
     )

time: 339 us -> 826 us (2.44)
  waiting for transfers between devices: 259 us -> 749 us
    reduce_scatter x0 -> x3, waiting for transfers between devices: none -> 626 us  [body(): lax.psum_scatter(term.astype(jnp.bfloat16), 'dp', scatter_dimension=0, ti...]
    unnamed x6 -> x7, waiting for transfers between devices: 141 us -> 0.11 us
  transfers between devices with their start and end apart: 5 -> 7, of which waited for: 5 -> 7; matrix products, arithmetic and copies ran while one was open for 9% -> 4% of each run, Pallas kernels for 0% -> 0%
where the time goes in v1:
time: 826 us
  waiting for transfers between devices  749 us (91%)
  matrix products  31 us (4%)
  local copies, waits for them, and re-layouts  21.4 us (3%)
  between operations  14.4 us (2%)
  other arithmetic  9.27 us (1%)
    reduce_scatter x3, waiting for transfers between devices, body(): lax.psum_scatter(term.astype(jnp.bfloat16), 'dp', scatter_dimension=0, ti...  626 us
    reduce_scatter x1, waiting for transfers between devices, body(): lax.psum_scatter(input_part.astype(jnp.bfloat16), 'tensor', scatter_dimen...  36.7 us
    reduce_scatter x1, waiting for transfers between devices, body(): lax.psum_scatter(mixed_part.astype(jnp.bfloat16), 'tensor', scatter_dimen...  35.4 us
    all_gather x1, waiting for transfers between devices, body(): lax.all_gather(grad_out, 'tensor', axis=1, tiled=True)  26.5 us
    all_gather x1, waiting for transfers between devices, body(): lax.all_gather(tokens, 'tensor', axis=1, tiled=True)  24.2 us
  transfers between devices with their start and end apart: 7, of which 7 were waited for; matrix products, arithmetic and copies ran while one was open for 4% of the time, Pallas kernels for 0%

profile of v1, /device:TPU:8, one launch (start us, length us, event | category | flops | bytes accessed | tf_op | source)
XLA Modules:
  0.0 825.7 jit_solution(16852433310537458351)
XLA Ops:
  7.2 1.7 copy.39
  9.0 1.7 copy.47
  10.7 0.0 reduce-scatter.10.cloned.1.call-start
  10.8 0.7 compare_and_fusion
  11.5 0.7 compare_and_fusion.2
  12.2 0.7 compare_and_fusion.1
  12.9 0.7 fusion.78
  13.6 0.7 fusion.79
  14.2 0.7 fusion.77
  14.9 24.2 %all-gather.3.cloned.1.call-done = bf16[128,4096]{0,1:T(8,128)(2,1)} async-done(((bf16[128,512]{0,1:T(8,128)(2,1)}), bf16[128,4096]{0,1:T(8,128)(2,1)}) %all-gather.3.cloned.1.call-update) | async-done | bytes 1048592 | tf_op jit(solution)/shard_map/all_gather | solution.py:45
  39.1 1.6 copy.40
  40.7 26.5 %all-gather.5.cloned.1.call-done = bf16[128,4096]{0,1:T(8,128)(2,1)} async-done(((bf16[128,512]{0,1:T(8,128)(2,1)}), bf16[128,4096]{0,1:T(8,128)(2,1)}) %all-gather.5.cloned.1.call-update) | async-done | bytes 1048592 | tf_op jit(solution)/shard_map/all_gather | solution.py:46
  67.2 2.3 copy.48
  69.5 1.7 gather_fusion.1
  71.2 1.7 gather_fusion
  72.8 3.0 gather_fusion.3
  75.8 0.5 convolution_bitcast_fusion.5
  76.3 2.2 fusion.10
  78.6 0.5 convolution_bitcast_fusion.4
  79.1 2.2 fusion.8
  81.4 0.9 convolution_bitcast_fusion.2
  82.3 2.2 fusion.4
  84.5 1.1 fusion.37
  85.6 1.7 gather_fusion.4
  87.2 3.2 multiply_convert_fusion.2
  90.5 0.2 reduce-scatter.14.cloned.1.call-start
  90.7 1.7 gather_fusion.2
  92.4 3.2 multiply_convert_fusion
  95.6 0.0 reduce-scatter.12.cloned.1.call-start
  95.7 1.6 gather_fusion.5
  97.3 3.3 multiply_convert_fusion.1
  100.6 0.0 reduce-scatter.6.cloned.1.call-start
  100.7 0.5 convolution_bitcast_fusion.3
  101.2 3.0 fusion.14
  104.2 1.4 copy.90
  105.7 2.3 convolution_bitcast_fusion
  108.0 0.9 convolution_bitcast_fusion.1
  108.9 3.0 fusion
  111.9 3.1 add_convert_fusion
  115.0 1.4 copy.89
  116.5 190.5 %reduce-scatter.10.cloned.1.call-done = bf16[1,128,128]{2,1,0:T(8,128)(2,1)} async-done(((bf16[32,128,128]{2,1,0:T(8,128)(2,1)}), bf16[1,128,128]{2,1,0:T(8,128)(2,1)}) %reduce-scatter.10.cloned.1.call-update) | async-done | bytes 32784 | tf_op jit(solution)/shard_map/reduce_scatter | solution.py:96
  307.0 1.4 bitcast_convert_fusion.2
  308.4 217.8 %reduce-scatter.14.cloned.1.call-done = bf16[1,128,128]{2,1,0:T(8,128)(2,1)} async-done(((bf16[32,128,128]{2,1,0:T(8,128)(2,1)}), bf16[1,128,128]{2,1,0:T(8,128)(2,1)}) %reduce-scatter.14.cloned.1.call-update) | async-done | bytes 32784 | tf_op jit(solution)/shard_map/reduce_scatter | solution.py:96
  526.2 1.4 bitcast_convert_fusion
  527.6 217.8 %reduce-scatter.12.cloned.1.call-done = bf16[1,128,128]{2,1,0:T(8,128)(2,1)} async-done(((bf16[32,128,128]{2,1,0:T(8,128)(2,1)}), bf16[1,128,128]{2,1,0:T(8,128)(2,1)}) %reduce-scatter.12.cloned.1.call-update) | async-done | bytes 32784 | tf_op jit(solution)/shard_map/reduce_scatter | solution.py:96
  745.4 1.4 bitcast_convert_fusion.1
  746.8 35.4 %reduce-scatter.6.cloned.1.call-done = bf16[128,512]{1,0:T(8,128)(2,1)} async-done(((bf16[128,4096]{1,0:T(8,128)(2,1)}), bf16[128,512]{1,0:T(8,128)(2,1)}) %reduce-scatter.6.cloned.1.call-update) | async-done | bytes 131088 | tf_op jit(solution)/shard_map/reduce_scatter | solution.py:72
  782.2 36.7 %reduce-scatter.8.cloned.1.call-done = bf16[128,512]{1,0:T(8,128)(2,1)} async-done(((bf16[128,4096]{1,0:T(8,128)(2,1)}), bf16[128,512]{1,0:T(8,128)(2,1)}) %reduce-scatter.8.cloned.1.call-update) | async-done | bytes 131088 | tf_op jit(solution)/shard_map/reduce_scatter | solution.py:100
  (40 shorter events, 0.3 us)
Async XLA Ops:
  7.2 74.2 %copy-start = (bf16[1,32,128,128]{3,2,1,0:T(8,128)(2,1)S(1)}, bf16[1,32,128,128]{3,2,1,0:T(8,128)(2,1)}, u32[]{:S(2)}) copy-start(bf16[1,32,128,128]{3,2,1,0:T(8,128)(2,1)} %param.19) | copy-start | bytes 3145732
  7.2 31.9 %all-gather.3.cloned.1.call-start = ((), (), s32[]{:S(2)}) async-start(), calls=%async_computation.5 | async-start | bytes 1179648 | tf_op jit(solution)/shard_map/all_gather | solution.py:45
  9.0 58.3 %all-gather.5.cloned.1.call-start = ((), (), s32[]{:S(2)}) async-start(), calls=%async_computation.7 | async-start | bytes 1179648 | tf_op jit(solution)/shard_map/all_gather | solution.py:46
  10.7 296.2 %reduce-scatter.10.cloned.1.call-start = ((), (), s32[]{:S(2)}) async-start(), calls=%async_computation.9 | async-start | bytes 1081344 | tf_op jit(solution)/shard_map/reduce_scatter | solution.py:96
  71.2 4.6 copy-start.2
  72.8 3.0 copy-start.8
  76.3 2.3 copy-start.1
  76.3 2.3 copy-start.5
  79.1 2.3 copy-start.6
  90.5 435.7 %reduce-scatter.14.cloned.1.call-start = ((), (), s32[]{:S(2)}) async-start(), calls=%async_computation.11 | async-start | bytes 1081344 | tf_op jit(solution)/shard_map/reduce_scatter | solution.py:96
  95.6 649.8 %reduce-scatter.12.cloned.1.call-start = ((), (), s32[]{:S(2)}) async-start(), calls=%async_computation.10 | async-start | bytes 1081344 | tf_op jit(solution)/shard_map/reduce_scatter | solution.py:96
  97.3 3.4 copy-start.7
  100.6 681.5 %reduce-scatter.6.cloned.1.call-start = ((), (), s32[]{:S(2)}) async-start(), calls=%async_computation.6 | async-start | bytes 1179648 | tf_op jit(solution)/shard_map/reduce_scatter | solution.py:72
  105.6 2.3 copy-start.3
  105.6 713.2 %reduce-scatter.8.cloned.1.call-start = ((), (), s32[]{:S(2)}) async-start(), calls=%async_computation.8 | async-start | bytes 1179648 | tf_op jit(solution)/shard_map/reduce_scatter | solution.py:100
  105.7 2.3 copy-start.4
Sparse Core Ops, SparseCore 0:
  10.4 28.6 all-gather.2
  41.5 25.6 all-gather.4
  90.6 216.3 reduce-scatter.9
  310.6 215.4 reduce-scatter.13
  529.8 215.5 reduce-scatter.11
  748.4 33.7 reduce-scatter.5
  785.3 33.5 reduce-scatter.7

commit v2 on v0

--- a/solution.py
+++ b/solution.py
@@ -38,13 +38,24 @@
     return product * weight[:, None, None]
 
 
+def gather_features(part, axis):
+    count = lax.axis_size(axis)
+    spread_out = jnp.broadcast_to(part[None], (count,) + part.shape)
+    pieces = lax.all_to_all(spread_out, axis, 0, 0, tiled=True)
+    return pieces.transpose(1, 0, 2).reshape(part.shape[0], count * part.shape[1])
+
+
+def scatter_features(full, axis):
+    count = lax.axis_size(axis)
+    pieces = lax.all_to_all(full.reshape(full.shape[0], count, -1), axis, 1, 1, tiled=True)
+    return pieces.astype(jnp.float32).sum(1).astype(jnp.bfloat16)
+
+
 def body(
     tokens, grad_out, gate_blocks, gate_values, up_blocks, up_values, down_blocks, down_values
 ):
-    gathered_x, gathered_dy = (
-        lax.all_gather(tokens, "tensor", axis=1, tiled=True),
-        lax.all_gather(grad_out, "tensor", axis=1, tiled=True),
-    )
+    gathered_x = gather_features(tokens, "tensor")
+    gathered_dy = gather_features(grad_out, "tensor")
     tok_rows, feature_width = gathered_x.shape
     block_size = gate_values.shape[-1]
     feature_count = feature_width // block_size
@@ -69,9 +80,7 @@
     )
     mixed_part = mixed_part.reshape(tok_rows, feature_width)
     upstream_rows = select(upstream, down_feat)
-    mixed = lax.psum_scatter(
-        mixed_part.astype(jnp.bfloat16), "tensor", scatter_dimension=1, tiled=True
-    )
+    mixed = scatter_features(mixed_part.astype(jnp.bfloat16), "tensor")
     hidden_grad = spread(
         backward_blocks(upstream_rows, down_values[0]), one_hot(down_hid, down_live, hidden_count)
     )
@@ -92,18 +101,13 @@
     gate_term = slot_term(gate_rows, gate_delta_rows, gate_live)
     up_term = slot_term(up_rows, up_delta_rows, up_live)
     down_term = slot_term(hidden_rows, upstream_rows, down_live)
-    combined = lax.psum_scatter(
-        jnp.stack([gate_term, up_term, down_term], axis=1).astype(jnp.bfloat16),
-        "dp",
-        scatter_dimension=0,
-        tiled=True,
-    ).astype(jnp.float32)
+    stacked = jnp.stack([gate_term, up_term, down_term], axis=1).astype(jnp.bfloat16)
+    combined = lax.all_to_all(stacked, "dp", 0, 0, tiled=True).astype(jnp.float32)
+    combined = combined.sum(0, keepdims=True)
     grad_gate = combined[None, :, 0]
     grad_up = combined[None, :, 1]
     grad_down = combined[None, :, 2]
-    grad_tokens = lax.psum_scatter(
-        input_part.astype(jnp.bfloat16), "tensor", scatter_dimension=1, tiled=True
-    )
+    grad_tokens = scatter_features(input_part.astype(jnp.bfloat16), "tensor")
     return (mixed, grad_tokens, grad_gate, grad_up, grad_down)
 
 

time: 339 us -> 205 us (0.60)
  waiting for transfers between devices: 259 us -> 107 us
  starting transfers between devices: 0.43 us -> 28.5 us
  between operations: 14.1 us -> 1.13 us
  local copies, waits for them, and re-layouts: 23 us -> 31.3 us
  matrix products: 33.4 us -> 27.4 us
    unnamed x6 -> x0, waiting for transfers between devices: 141 us -> none
    all_to_all x0 -> x5, waiting for transfers between devices: none -> 107 us  [the longest x1 66.7 us: body(): lax.all_to_all(stacked, 'dp', 0, 0, tiled=True).astype(jnp.float32)]
    reduce_scatter x2 -> x0, waiting for transfers between devices: 70.8 us -> none  [the longest x1 36.6 us: body(): lax.psum_scatter(mixed_part.astype(jnp.bfloat16), 'tensor', scatter_dimen...]
    all_gather x2 -> x0, waiting for transfers between devices: 47.4 us -> none  [the longest x1 24.2 us: body(): lax.all_gather(tokens, 'tensor', axis=1, tiled=True)]
    all_to_all x0 -> x5, starting transfers between devices: none -> 28.5 us  [the longest x1 11.7 us: body(): lax.all_to_all(stacked, 'dp', 0, 0, tiled=True).astype(jnp.float32)]
    convert_element_type x0 -> x4, local copies, waits for them, and re-layouts: none -> 9.12 us  [the longest x2 5.06 us: body(): mixed = scatter_features(mixed_part.astype(jnp.bfloat16), 'tensor')]
    dot_general x3, matrix products: 8.89 us -> 2.01 us  [slot_term(): jnp.einsum('tsk,tsn->skn', left, right, preferred_element_type=jnp.float32)]
    reduce_sum x0 -> x3, other arithmetic: none -> 6.6 us  [the longest x2 4.12 us: scatter_features(): return pieces.astype(jnp.float32).sum(1).astype(jnp.bfloat16)]
  transfers between devices with their start and end apart: 5 -> 5, of which waited for: 5 -> 4; matrix products, arithmetic and copies ran while one was open for 9% -> 13% of each run, Pallas kernels for 0% -> 0%
where the time goes in v2:
time: 205 us; the launch traced here: 203 us
  waiting for transfers between devices  107 us (52%)
  local copies, waits for them, and re-layouts  31.3 us (15%)
  starting transfers between devices  28.5 us (14%)
  matrix products  27.4 us (13%)
  other arithmetic  8.11 us (4%)
    all_to_all x1, waiting for transfers between devices, body(): lax.all_to_all(stacked, 'dp', 0, 0, tiled=True).astype(jnp.float32)  66.7 us
    all_to_all x2, waiting for transfers between devices, gather_features(): pieces = lax.all_to_all(spread_out, axis, 0, 0, tiled=True)  30.1 us
    dot_general x6, matrix products, spread(): jnp.einsum('tsn,sc->tcn', product, table, precision=lax.Precision.HIGHEST)  17 us
    all_to_all x1, starting transfers between devices, body(): lax.all_to_all(stacked, 'dp', 0, 0, tiled=True).astype(jnp.float32)  11.7 us
    gather x6, local copies, waits for them, and re-layouts, select(): return jnp.take(source, position, axis=1)  10.3 us
    all_to_all x2, waiting for transfers between devices, scatter_features(): lax.all_to_all(full.reshape(full.shape[0], count, -1), axis, 1, 1, tiled=...  9.86 us
    all_to_all x2, starting transfers between devices, scatter_features(): lax.all_to_all(full.reshape(full.shape[0], count, -1), axis, 1, 1, tiled=...  8.94 us
    all_to_all x2, starting transfers between devices, gather_features(): pieces = lax.all_to_all(spread_out, axis, 0, 0, tiled=True)  7.86 us
  transfers between devices with their start and end apart: 5, of which 4 were waited for; matrix products, arithmetic and copies ran while one was open for 13% of the time, Pallas kernels for 0%

profile of v2, /device:TPU:8, one launch (start us, length us, event | category | flops | bytes accessed | tf_op | source)
XLA Modules:
  0.0 203.1 jit_solution(11530250538652315190)
XLA Ops:
  0.7 1.1 copy.56
  1.8 1.1 broadcast_in_dim.22
  2.9 4.3 %all-to-all-start.2 = ((bf16[8,128,512]{1,2,0:T(8,128)(2,1)}), bf16[8,128,512]{1,2,0:T(8,128)(2,1)S(1)}, u32[]{:S(2)}, u32[]{:S(2)}) async-start(bf16[8,128,512]{1,2,0:T(8,128)(2,1)} %broadcast_in_dim.22), calls=%async_computation.2 | async-start | bytes 2097152 | tf_op jit(solution)/shard_map/all_to_all | solution.py:44
  7.6 15.6 %all-to-all-done.2 = bf16[8,128,512]{1,2,0:T(8,128)(2,1)S(1)} async-done(((bf16[8,128,512]{1,2,0:T(8,128)(2,1)}), bf16[8,128,512]{1,2,0:T(8,128)(2,1)S(1)}, u32[]{:S(2)}, u32[]{:S(2)}) %all-to-all-start.2) | async-done | bytes 1048608 | tf_op jit(solution)/shard_map/all_to_all | solution.py:44
  23.2 1.1 broadcast_in_dim.21
  24.3 3.6 %all-to-all-start = ((bf16[8,128,512]{1,2,0:T(8,128)(2,1)}), bf16[8,128,512]{1,2,0:T(8,128)(2,1)S(1)}, u32[]{:S(2)}, u32[]{:S(2)}) async-start(bf16[8,128,512]{1,2,0:T(8,128)(2,1)} %broadcast_in_dim.21), calls=%async_computation | async-start | bytes 2097152 | tf_op jit(solution)/shard_map/all_to_all | solution.py:44
  27.9 1.3 copy.57
  29.3 14.5 %all-to-all-done = bf16[8,128,512]{1,2,0:T(8,128)(2,1)S(1)} async-done(((bf16[8,128,512]{1,2,0:T(8,128)(2,1)}), bf16[8,128,512]{1,2,0:T(8,128)(2,1)S(1)}, u32[]{:S(2)}, u32[]{:S(2)}) %all-to-all-start) | async-done | bytes 1048608 | tf_op jit(solution)/shard_map/all_to_all | solution.py:44
  43.7 1.0 copy-done.12
  44.7 1.6 copy.48
  46.3 1.7 gather_fusion.1
  48.0 1.6 gather_fusion
  49.7 2.0 gather_fusion.3
  51.7 2.1 %convolution_bitcast_fusion.5 = f32[128,32,128]{2,0,1:T(8,128)S(1)} fusion(bf16[1,32,128,128]{3,2,1,0:T(8,128)(2,1)S(1)} %copy-done.2, bf16[32,128,128]{2,1,0:T(8,128)(2,1)} %gather_fusion, pred[32]{0:T(512)(128)(4,1)S(1)} %get-tuple-element.27), kind=kOutput, calls=%fused_computation.29 | convolution fusion | flops 134742016 | bytes 4194336 | tf_op jit(solution)/shard_map/tsk,skn->tsn/dot_general | solution.py:29
  53.8 2.2 %fusion.10 = f32[14,128,128]{2,0,1:T(8,128)S(1)} fusion(f32[128,32,128]{2,0,1:T(8,128)S(1)} %convolution_bitcast_fusion.5, f32[32]{0:T(128)S(1)} %fusion.87, s32[32]{0:T(128)S(1)} %get-tuple-element.8), kind=kOutput, calls=%fused_computation.18 | convolution fusion | flops 88081280 | bytes 3014912 | tf_op jit(solution)/shard_map/tsn,sc->tcn/dot_general | solution.py:21
  56.1 0.5 convolution_bitcast_fusion.4
  56.6 2.2 %fusion.8 = f32[14,128,128]{2,0,1:T(8,128)S(1)} fusion(f32[128,32,128]{2,0,1:T(8,128)S(1)} %convolution_bitcast_fusion.4, f32[32]{0:T(128)S(1)} %fusion.88, s32[32]{0:T(128)S(1)} %get-tuple-element.10), kind=kOutput, calls=%fused_computation.16 | convolution fusion | flops 88081280 | bytes 3014912 | tf_op jit(solution)/shard_map/tsn,sc->tcn/dot_general | solution.py:21
  58.8 0.9 convolution_bitcast_fusion.2
  59.7 2.2 %fusion.4 = f32[14,128,128]{2,0,1:T(8,128)S(1)} fusion(f32[128,32,128]{2,0,1:T(8,128)S(1)} %convolution_bitcast_fusion.2, f32[32]{0:T(128)S(1)} %fusion.86, s32[32]{0:T(128)S(1)} %get-tuple-element.26), kind=kOutput, calls=%fused_computation.12 | convolution fusion | flops 88081280 | bytes 3014912 | tf_op jit(solution)/shard_map/tsn,sc->tcn/dot_general | solution.py:21
  62.0 1.1 fusion.46
  63.0 1.7 gather_fusion.2
  64.7 1.7 convolution_bitcast_fusion.3
  66.4 4.2 %fusion.17 = bf16[128,32,128]{2,1,0:T(8,128)(2,1)} fusion(f32[128,32,128]{2,0,1:T(8,128)S(1)} %convolution_bitcast_fusion.3, f32[32]{0:T(128)S(1)} %fusion.86, s32[32]{0:T(128)S(1)} %get-tuple-element.12), kind=kOutput, calls=%fused_computation.31 | convolution fusion | flops 201852928 | bytes 3145984 | tf_op jit(solution)/shard_map/tsn,sc->tcn/dot_general | solution.py:21
  70.6 2.5 %convert_element_type.94 = bf16[128,8,512]{2,1,0:T(8,128)(2,1)} reshape(bf16[128,32,128]{2,1,0:T(8,128)(2,1)} %fusion.17) | data formatting | bytes 2097152 | tf_op jit(solution)/shard_map/convert_element_type | solution.py:83
  73.0 2.6 %copy.55 = bf16[128,8,512]{2,0,1:T(8,128)(2,1)} copy(bf16[128,8,512]{2,1,0:T(8,128)(2,1)} %convert_element_type.94) | data formatting | bytes 2097152 | tf_op jit(solution)/shard_map/convert_element_type | solution.py:83
  75.6 4.2 %all-to-all-start.1 = ((bf16[128,8,512]{2,0,1:T(8,128)(2,1)}), bf16[128,8,512]{2,0,1:T(8,128)(2,1)}, u32[]{:S(2)}, u32[]{:S(2)}) async-start(bf16[128,8,512]{2,0,1:T(8,128)(2,1)} %copy.55), calls=%async_computation.1 | async-start | bytes 2097152 | tf_op jit(solution)/shard_map/all_to_all | solution.py:50
  79.9 1.7 gather_fusion.4
  81.5 1.7 gather_fusion.5
  83.2 2.3 %convolution_bitcast_fusion = f32[128,32,128]{2,0,1:T(8,128)S(1)} fusion(bf16[1,32,128,128]{3,2,1,0:T(8,128)(2,1)S(1)} %copy-done.1, bf16[32,128,128]{2,1,0:T(8,128)(2,1)} %gather_fusion.5, pred[32]{0:T(512)(128)(4,1)S(1)} %get-tuple-element.9), kind=kOutput, calls=%fused_computation.24 | convolution fusion | flops 134742016 | bytes 4194336 | tf_op jit(solution)/shard_map/tsn,skn->tsk/dot_general | solution.py:33
  85.5 0.9 convolution_bitcast_fusion.1
  86.4 3.0 %fusion = f32[32,128,128]{2,0,1:T(8,128)S(1)} fusion(f32[128,32,128]{2,0,1:T(8,128)S(1)} %convolution_bitcast_fusion, f32[32]{0:T(128)S(1)} %fusion.88, s32[32]{0:T(128)S(1)} %get-tuple-element.30), kind=kOutput, calls=%fused_computation.8 | convolution fusion | flops 201328640 | bytes 4194560 | tf_op jit(solution)/shard_map/tsn,sc->tcn/dot_general | solution.py:21
  89.4 3.1 %fusion.20 = bf16[128,32,128]{2,1,0:T(8,128)(2,1)S(1)} fusion(f32[32,128,128]{2,0,1:T(8,128)S(1)} %fusion, f32[128,32,128]{2,0,1:T(8,128)S(1)} %convolution_bitcast_fusion.1, f32[32]{0:T(128)S(1)} %fusion.87, s32[32]{0:T(128)S(1)} %get-tuple-element.28), kind=kOutput, calls=%fused_computation.32 | convolution fusion | flops 202377216 | bytes 5243136 | tf_op jit(solution)/shard_map/tsn,sc->tcn/dot_general | solution.py:21
  92.5 1.5 convert_element_type.99
  94.0 2.6 %copy.62 = bf16[128,8,512]{2,0,1:T(8,128)(2,1)} copy(bf16[128,8,512]{2,1,0:T(8,128)(2,1)} %convert_element_type.99) | data formatting | bytes 2097152 | tf_op jit(solution)/shard_map/convert_element_type | solution.py:110
  96.6 4.7 %all-to-all-start.3 = ((bf16[128,8,512]{2,0,1:T(8,128)(2,1)}), bf16[128,8,512]{2,0,1:T(8,128)(2,1)}, u32[]{:S(2)}, u32[]{:S(2)}) async-start(bf16[128,8,512]{2,0,1:T(8,128)(2,1)} %copy.62), calls=%async_computation.3 | async-start | bytes 2097152 | tf_op jit(solution)/shard_map/all_to_all | solution.py:50
  101.3 0.7 fusion.23
  102.0 0.5 copy-done.7
  102.9 0.7 fusion.25
  103.5 0.5 copy-done.5
  104.4 0.7 fusion.24
  105.4 2.1 %copy.66 = bf16[32,3,128,128]{3,2,1,0:T(8,128)(2,1)} copy(bf16[32,3,128,128]{3,2,0,1:T(8,128)(2,1)S(1)} %pad_maximum_fusion) | data formatting | bytes 6291456 | tf_op jit(solution)/shard_map/stack | solution.py:104
  107.5 9.9 %all-to-all-done.3 = bf16[128,8,512]{2,0,1:T(8,128)(2,1)} async-done(((bf16[128,8,512]{2,0,1:T(8,128)(2,1)}), bf16[128,8,512]{2,0,1:T(8,128)(2,1)}, u32[]{:S(2)}, u32[]{:S(2)}) %all-to-all-start.3) | async-done | bytes 1048608 | tf_op jit(solution)/shard_map/all_to_all | solution.py:50
  117.3 11.7 %all-to-all-start.4 = ((bf16[32,3,128,128]{3,2,1,0:T(8,128)(2,1)}), bf16[32,3,128,128]{3,2,1,0:T(8,128)(2,1)}, u32[]{:S(2)}, u32[]{:S(2)}) async-start(bf16[32,3,128,128]{3,2,1,0:T(8,128)(2,1)} %copy.66), calls=%async_computation.4 | async-start | bytes 6291456 | tf_op jit(solution)/shard_map/all_to_all | solution.py:105
  129.1 2.1 %reduce_sum.33 = bf16[128,512]{1,0:T(8,128)(2,1)} reduce(bf16[128,8,512]{2,0,1:T(8,128)(2,1)} %all-to-all-done.1, bf16[]{:T(256)} %constant.109.clone.1), dimensions={1}, to_apply=%region_0.3 | reduce | flops 458752 | bytes 1179650 | tf_op jit(solution)/shard_map/reduce_sum | solution.py:51
  131.2 2.1 %reduce_sum.34 = bf16[128,512]{1,0:T(8,128)(2,1)} reduce(bf16[128,8,512]{2,0,1:T(8,128)(2,1)} %all-to-all-done.3, bf16[]{:T(256)} %constant.109.clone.1), dimensions={1}, to_apply=%region_1.4 | reduce | flops 458752 | bytes 1179650 | tf_op jit(solution)/shard_map/reduce_sum | solution.py:51
  133.2 66.7 %all-to-all-done.4 = bf16[32,3,128,128]{3,2,1,0:T(8,128)(2,1)} async-done(((bf16[32,3,128,128]{3,2,1,0:T(8,128)(2,1)}), bf16[32,3,128,128]{3,2,1,0:T(8,128)(2,1)}, u32[]{:S(2)}, u32[]{:S(2)}) %all-to-all-start.4) | async-done | bytes 3145760 | tf_op jit(solution)/shard_map/all_to_all | solution.py:105
  199.9 2.5 %convert_reduce_fusion = f32[3,128,128]{2,1,0:T(8,128)S(1)} fusion(bf16[32,3,128,128]{3,2,1,0:T(8,128)(2,1)} %all-to-all-done.4), kind=kLoop, calls=%fused_computation.6 | loop fusion | flops 3096576 | bytes 3342336 | tf_op jit(solution)/shard_map/reduce_sum | solution.py:106
  202.4 0.7 fusion.107
  (52 shorter events, 1.3 us)
Async XLA Ops:
  0.6 58.2 %copy-start = (bf16[1,32,128,128]{3,2,1,0:T(8,128)(2,1)S(1)}, bf16[1,32,128,128]{3,2,1,0:T(8,128)(2,1)}, u32[]{:S(2)}) copy-start(bf16[1,32,128,128]{3,2,1,0:T(8,128)(2,1)} %param.19) | copy-start | bytes 3145732
  0.6 6.6 %copy-start.15 = (s32[1,32]{1,0:T(1,128)S(1)}, s32[1,32]{1,0:T(1,128)}, u32[]{:S(2)}) copy-start(s32[1,32]{1,0:T(1,128)} %param.16) | copy-start | bytes 388
  0.7 6.6 %copy-start.16 = (s32[1,32]{1,0:T(1,128)S(1)}, s32[1,32]{1,0:T(1,128)}, u32[]{:S(2)}) copy-start(s32[1,32]{1,0:T(1,128)} %param.18) | copy-start | bytes 388
  0.7 6.7 %copy-start.13 = (bf16[128,512]{1,0:T(8,128)(2,1)S(1)}, bf16[128,512]{1,0:T(8,128)(2,1)}, u32[]{:S(2)}) copy-start(bf16[128,512]{1,0:T(8,128)(2,1)} %param.12) | copy-start | bytes 393220
  0.7 6.8 %copy-start.14 = (s32[1,32]{1,0:T(1,128)S(1)}, s32[1,32]{1,0:T(1,128)}, u32[]{:S(2)}) copy-start(s32[1,32]{1,0:T(1,128)} %param.14) | copy-start | bytes 388
  2.9 20.2 %all-to-all-start.2 = ((bf16[8,128,512]{1,2,0:T(8,128)(2,1)}), bf16[8,128,512]{1,2,0:T(8,128)(2,1)S(1)}, u32[]{:S(2)}, u32[]{:S(2)}) async-start(bf16[8,128,512]{1,2,0:T(8,128)(2,1)} %broadcast_in_dim.22), calls=%async_computation.2 | async-start | bytes 2097152 | tf_op jit(solution)/shard_map/all_to_all | solution.py:44
  24.3 19.4 %all-to-all-start = ((bf16[8,128,512]{1,2,0:T(8,128)(2,1)}), bf16[8,128,512]{1,2,0:T(8,128)(2,1)S(1)}, u32[]{:S(2)}, u32[]{:S(2)}) async-start(bf16[8,128,512]{1,2,0:T(8,128)(2,1)} %broadcast_in_dim.21), calls=%async_computation | async-start | bytes 2097152 | tf_op jit(solution)/shard_map/all_to_all | solution.py:44
  43.7 1.0 copy-start.12
  48.0 3.6 %copy-start.2 = (bf16[1,32,128,128]{3,2,1,0:T(8,128)(2,1)S(1)}, bf16[1,32,128,128]{3,2,1,0:T(8,128)(2,1)}, u32[]{:S(2)}) copy-start(bf16[1,32,128,128]{3,2,1,0:T(8,128)(2,1)} %param.15) | copy-start | bytes 3145732
  51.6 7.2 %copy-start.6 = (bf16[32,128,128]{2,1,0:T(8,128)(2,1)}, bf16[32,128,128]{2,1,0:T(8,128)(2,1)S(1)}, u32[]{:S(2)}) copy-start(bf16[32,128,128]{2,1,0:T(8,128)(2,1)S(1)} %gather_fusion.3) | copy-start | bytes 3145732
  53.8 2.3 %copy-start.1 = (bf16[1,32,128,128]{3,2,1,0:T(8,128)(2,1)S(1)}, bf16[1,32,128,128]{3,2,1,0:T(8,128)(2,1)}, u32[]{:S(2)}) copy-start(bf16[1,32,128,128]{3,2,1,0:T(8,128)(2,1)} %param.17) | copy-start | bytes 3145732
  53.8 2.3 %copy-start.4 = (bf16[32,128,128]{2,1,0:T(8,128)(2,1)S(1)}, bf16[32,128,128]{2,1,0:T(8,128)(2,1)}, u32[]{:S(2)}) copy-start(bf16[32,128,128]{2,1,0:T(8,128)(2,1)} %gather_fusion.1) | copy-start | bytes 3145732
  75.6 21.0 %all-to-all-start.1 = ((bf16[128,8,512]{2,0,1:T(8,128)(2,1)}), bf16[128,8,512]{2,0,1:T(8,128)(2,1)}, u32[]{:S(2)}, u32[]{:S(2)}) async-start(bf16[128,8,512]{2,0,1:T(8,128)(2,1)} %copy.55), calls=%async_computation.1 | async-start | bytes 2097152 | tf_op jit(solution)/shard_map/all_to_all | solution.py:50
  83.2 2.3 %copy-start.3 = (bf16[1,32,128,128]{3,2,1,0:T(8,128)(2,1)S(1)}, bf16[1,32,128,128]{3,2,1,0:T(8,128)(2,1)}, u32[]{:S(2)}) copy-start(bf16[1,32,128,128]{3,2,1,0:T(8,128)(2,1)} %param.15) | copy-start | bytes 3145732
  83.2 2.3 %copy-start.11 = (bf16[32,128,128]{2,1,0:T(8,128)(2,1)S(1)}, bf16[32,128,128]{2,1,0:T(8,128)(2,1)}, u32[]{:S(2)}) copy-start(bf16[32,128,128]{2,1,0:T(8,128)(2,1)} %gather_fusion.4) | copy-start | bytes 3145732
  94.0 7.3 %copy-start.8 = (bf16[32,128,128]{2,1,0:T(8,128)(2,1)S(1)}, bf16[32,128,128]{2,1,0:T(8,128)(2,1)}, u32[]{:S(2)}) copy-start(bf16[32,128,128]{2,1,0:T(8,128)(2,1)} %gather_fusion) | copy-start | bytes 3145732
  96.6 20.7 %all-to-all-start.3 = ((bf16[128,8,512]{2,0,1:T(8,128)(2,1)}), bf16[128,8,512]{2,0,1:T(8,128)(2,1)}, u32[]{:S(2)}, u32[]{:S(2)}) async-start(bf16[128,8,512]{2,0,1:T(8,128)(2,1)} %copy.62), calls=%async_computation.3 | async-start | bytes 2097152 | tf_op jit(solution)/shard_map/all_to_all | solution.py:50
  101.3 1.2 copy-start.7
  101.3 1.5 copy-start.9
  102.9 1.2 copy-start.5
  102.9 1.5 copy-start.10
  117.3 82.6 %all-to-all-start.4 = ((bf16[32,3,128,128]{3,2,1,0:T(8,128)(2,1)}), bf16[32,3,128,128]{3,2,1,0:T(8,128)(2,1)}, u32[]{:S(2)}, u32[]{:S(2)}) async-start(bf16[32,3,128,128]{3,2,1,0:T(8,128)(2,1)} %copy.66), calls=%async_computation.4 | async-start | bytes 6291456 | tf_op jit(solution)/shard_map/all_to_all | solution.py:105

commit v3 on v2

--- a/solution.py
+++ b/solution.py
@@ -1,6 +1,7 @@
 import jax
 import jax.numpy as jnp
 from jax import lax
+from jax.sharding import Mesh
 from jax.sharding import PartitionSpec as P
 
 FF = 14336
@@ -38,11 +39,20 @@
     return product * weight[:, None, None]
 
 
-def gather_features(part, axis):
+def gather_features(parts, axis):
     count = lax.axis_size(axis)
-    spread_out = jnp.broadcast_to(part[None], (count,) + part.shape)
+    spread_out = jnp.broadcast_to(parts[None], (count,) + parts.shape)
     pieces = lax.all_to_all(spread_out, axis, 0, 0, tiled=True)
-    return pieces.transpose(1, 0, 2).reshape(part.shape[0], count * part.shape[1])
+    rows, width = parts.shape[-2:]
+    return pieces.transpose(1, 2, 0, 3).reshape(parts.shape[0], rows, count * width)
+
+
+def reduce_slots(stacked, outer, inner):
+    outer_count, inner_count = lax.axis_size(outer), lax.axis_size(inner)
+    grid = stacked.reshape((outer_count, inner_count) + stacked.shape[1:])
+    grid = lax.all_to_all(grid, inner, 1, 1, tiled=True).astype(jnp.float32).sum(1)
+    grid = lax.all_to_all(grid.astype(jnp.bfloat16), outer, 0, 0, tiled=True)
+    return grid.astype(jnp.float32).sum(0)
 
 
 def scatter_features(full, axis):
@@ -54,8 +64,7 @@
 def body(
     tokens, grad_out, gate_blocks, gate_values, up_blocks, up_values, down_blocks, down_values
 ):
-    gathered_x = gather_features(tokens, "tensor")
-    gathered_dy = gather_features(grad_out, "tensor")
+    gathered_x, gathered_dy = gather_features(jnp.stack([tokens, grad_out]), "tensor")
     tok_rows, feature_width = gathered_x.shape
     block_size = gate_values.shape[-1]
     feature_count = feature_width // block_size
@@ -102,8 +111,7 @@
     up_term = slot_term(up_rows, up_delta_rows, up_live)
     down_term = slot_term(hidden_rows, upstream_rows, down_live)
     stacked = jnp.stack([gate_term, up_term, down_term], axis=1).astype(jnp.bfloat16)
-    combined = lax.all_to_all(stacked, "dp", 0, 0, tiled=True).astype(jnp.float32)
-    combined = combined.sum(0, keepdims=True)
+    combined = reduce_slots(stacked, "z", "y")[None]
     grad_gate = combined[None, :, 0]
     grad_up = combined[None, :, 1]
     grad_down = combined[None, :, 2]
@@ -112,9 +120,15 @@
 
 
 def solution(mesh):
+    dp_count, tensor_count = mesh.devices.shape
+    y_count = len({device.coords[1] for device in mesh.devices[:, 0]})
+    split_mesh = Mesh(
+        mesh.devices.reshape(dp_count // y_count, y_count, tensor_count), ("z", "y", "tensor")
+    )
+    dp = ("z", "y")
     in_specs = (
-        P("dp", "tensor"),
-        P("dp", "tensor"),
+        P(dp, "tensor"),
+        P(dp, "tensor"),
         P("tensor", None),
         P("tensor", None, None, None),
         P("tensor", None),
@@ -123,10 +137,12 @@
         P("tensor", None, None, None),
     )
     out_specs = (
-        P("dp", "tensor"),
-        P("dp", "tensor"),
-        P("tensor", "dp", None, None),
-        P("tensor", "dp", None, None),
-        P("tensor", "dp", None, None),
+        P(dp, "tensor"),
+        P(dp, "tensor"),
+        P("tensor", dp, None, None),
+        P("tensor", dp, None, None),
+        P("tensor", dp, None, None),
     )
-    return jax.shard_map(body, mesh=mesh, in_specs=in_specs, out_specs=out_specs, check_vma=False)
+    return jax.shard_map(
+        body, mesh=split_mesh, in_specs=in_specs, out_specs=out_specs, check_vma=False
+    )

time: 205 us -> 183 us (0.89)
  waiting for transfers between devices: 107 us -> 87.5 us
  local copies, waits for them, and re-layouts: 31.3 us -> 27.1 us
  starting transfers between devices: 28.5 us -> 25.8 us
  matrix products: 27.4 us -> 29.7 us
    all_to_all x1 -> x2, waiting for transfers between devices: 66.7 us -> 44.4 us  [the longest x1 24.5 us: reduce_slots(): lax.all_to_all(grid, inner, 1, 1, tiled=True).astype(jnp.float32).sum(1)]
    all_to_all x2, waiting for transfers between devices: 9.86 us -> 16.1 us  [scatter_features(): lax.all_to_all(full.reshape(full.shape[0], count, -1), axis, 1, 1, tiled=...]
    dot_general x3, matrix products: 2.01 us -> 5.65 us  [slot_term(): jnp.einsum('tsk,tsn->skn', left, right, preferred_element_type=jnp.float32)]
    all_to_all x2 -> x1, starting transfers between devices: 7.86 us -> 4.43 us  [gather_features(): pieces = lax.all_to_all(spread_out, axis, 0, 0, tiled=True)]
    unnamed x36, local copies, waits for them, and re-layouts: 3.99 us -> 0.61 us
    all_to_all x2 -> x1, waiting for transfers between devices: 30.1 us -> 26.9 us  [gather_features(): pieces = lax.all_to_all(spread_out, axis, 0, 0, tiled=True)]
    all_to_all x1 -> x2, starting transfers between devices: 11.7 us -> 13.6 us  [the longest x1 7.6 us: reduce_slots(): grid = lax.all_to_all(grid.astype(jnp.bfloat16), outer, 0, 0, tiled=True)]
  transfers between devices with their start and end apart: 5 -> 5, of which waited for: 4 -> 5; matrix products, arithmetic and copies ran while one was open for 13% -> 16% of each run, Pallas kernels for 0% -> 0%
where the time goes in v3:
time: 183 us; the launch traced here: 180 us
  waiting for transfers between devices  87.5 us (48%)
  matrix products  29.7 us (16%)
  local copies, waits for them, and re-layouts  27.1 us (15%)
  starting transfers between devices  25.8 us (14%)
  other arithmetic  9.04 us (5%)
    all_to_all x1, waiting for transfers between devices, gather_features(): pieces = lax.all_to_all(spread_out, axis, 0, 0, tiled=True)  26.9 us
    all_to_all x1, waiting for transfers between devices, reduce_slots(): lax.all_to_all(grid, inner, 1, 1, tiled=True).astype(jnp.float32).sum(1)  24.5 us
    all_to_all x1, waiting for transfers between devices, reduce_slots(): grid = lax.all_to_all(grid.astype(jnp.bfloat16), outer, 0, 0, tiled=True)  19.9 us
    dot_general x6, matrix products, spread(): jnp.einsum('tsn,sc->tcn', product, table, precision=lax.Precision.HIGHEST)  17 us
    all_to_all x2, waiting for transfers between devices, scatter_features(): lax.all_to_all(full.reshape(full.shape[0], count, -1), axis, 1, 1, tiled=...  16.1 us
    gather x6, local copies, waits for them, and re-layouts, select(): return jnp.take(source, position, axis=1)  11.5 us
    all_to_all x2, starting transfers between devices, scatter_features(): lax.all_to_all(full.reshape(full.shape[0], count, -1), axis, 1, 1, tiled=...  7.8 us
    all_to_all x1, starting transfers between devices, reduce_slots(): grid = lax.all_to_all(grid.astype(jnp.bfloat16), outer, 0, 0, tiled=True)  7.6 us
  transfers between devices with their start and end apart: 5, of which 5 were waited for; matrix products, arithmetic and copies ran while one was open for 16% of the time, Pallas kernels for 0%

profile of v3, /device:TPU:8, one launch (start us, length us, event | category | flops | bytes accessed | tf_op | source)
XLA Modules:
  0.0 180.2 jit_solution(16797438349867666378)
XLA Ops:
  0.6 1.1 pad_maximum_fusion.1
  1.9 1.7 broadcast_in_dim.22
  3.7 4.4 %all-to-all-start = ((bf16[8,2,128,512]{2,3,1,0:T(8,128)(2,1)}), bf16[8,2,128,512]{2,3,1,0:T(8,128)(2,1)S(1)}, u32[]{:S(2)}, u32[]{:S(2)}) async-start(bf16[8,2,128,512]{2,3,1,0:T(8,128)(2,1)} %broadcast_in_dim.22), calls=%async_computation | async-start | bytes 4194304 | tf_op jit(solution)/shard_map/all_to_all | solution.py:45
  8.3 26.9 %all-to-all-done = bf16[8,2,128,512]{2,3,1,0:T(8,128)(2,1)S(1)} async-done(((bf16[8,2,128,512]{2,3,1,0:T(8,128)(2,1)}), bf16[8,2,128,512]{2,3,1,0:T(8,128)(2,1)S(1)}, u32[]{:S(2)}, u32[]{:S(2)}) %all-to-all-start) | async-done | bytes 2097184 | tf_op jit(solution)/shard_map/all_to_all | solution.py:45
  35.6 1.3 copy.83
  36.9 0.7 copy.75
  37.5 1.7 gather_fusion.1
  39.2 1.6 gather_fusion
  40.9 3.0 %gather_fusion.3 = bf16[32,128,128]{2,1,0:T(8,128)(2,1)} fusion(bf16[128,32,128]{2,0,1:T(8,128)(2,1)} %copy.83, s32[1024]{0:T(1024)S(1)} %pad_clamp_fusion.2), kind=kCustom, calls=%fused_computation.3.clone | custom fusion | bytes 2097280 | tf_op jit(solution)/shard_map/jit(_take)/gather | solution.py:26
  43.8 0.5 convolution_bitcast_fusion.5
  44.4 2.2 %fusion.10 = f32[14,128,128]{2,0,1:T(8,128)S(1)} fusion(f32[128,32,128]{2,0,1:T(8,128)S(1)} %convolution_bitcast_fusion.5, f32[32]{0:T(128)S(1)} %fusion.84, s32[32]{0:T(128)S(1)} %get-tuple-element.8), kind=kOutput, calls=%fused_computation.17 | convolution fusion | flops 88081280 | bytes 3014912 | tf_op jit(solution)/shard_map/tsn,sc->tcn/dot_general | solution.py:22
  46.6 0.5 convolution_bitcast_fusion.4
  47.2 2.2 %fusion.8 = f32[14,128,128]{2,0,1:T(8,128)S(1)} fusion(f32[128,32,128]{2,0,1:T(8,128)S(1)} %convolution_bitcast_fusion.4, f32[32]{0:T(128)S(1)} %fusion.85, s32[32]{0:T(128)S(1)} %get-tuple-element.10), kind=kOutput, calls=%fused_computation.15 | convolution fusion | flops 88081280 | bytes 3014912 | tf_op jit(solution)/shard_map/tsn,sc->tcn/dot_general | solution.py:22
  49.4 0.9 convolution_bitcast_fusion.2
  50.3 2.2 %fusion.4 = f32[14,128,128]{2,0,1:T(8,128)S(1)} fusion(f32[128,32,128]{2,0,1:T(8,128)S(1)} %convolution_bitcast_fusion.2, f32[32]{0:T(128)S(1)} %fusion.83, s32[32]{0:T(128)S(1)} %get-tuple-element.28), kind=kOutput, calls=%fused_computation.11 | convolution fusion | flops 88081280 | bytes 3014912 | tf_op jit(solution)/shard_map/tsn,sc->tcn/dot_general | solution.py:22
  52.6 2.0 %fusion.43 = (bf16[128,14,128]{2,0,1:T(8,128)(2,1)}, bf16[128,14,128]{2,0,1:T(8,128)(2,1)S(1)}, bf16[128,14,128]{2,0,1:T(8,128)(2,1)}) fusion(f32[14,128,128]{2,0,1:T(8,128)S(1)} %fusion.4, f32[14,128,128]{2,0,1:T(8,128)S(1)} %fusion.8, f32[14,128,128]{2,0,1:T(8,128)S(1)} %fusion.10), kind=kLoop, calls=%fused_computation.62 | loop fusion | flops 3440640 | bytes 4128768 | tf_op jit(solution)/shard_map/convert_element_type | solution.py:96
  54.6 1.7 gather_fusion.2
  56.2 1.7 convolution_bitcast_fusion.3
  58.0 4.1 %fusion.17 = bf16[128,32,128]{2,1,0:T(8,128)(2,1)} fusion(f32[128,32,128]{2,0,1:T(8,128)S(1)} %convolution_bitcast_fusion.3, f32[32]{0:T(128)S(1)} %fusion.83, s32[32]{0:T(128)S(1)} %get-tuple-element.12), kind=kOutput, calls=%fused_computation.32 | convolution fusion | flops 201852928 | bytes 3145984 | tf_op jit(solution)/shard_map/tsn,sc->tcn/dot_general | solution.py:22
  62.1 2.5 %convert_element_type.97 = bf16[128,8,512]{2,1,0:T(8,128)(2,1)} reshape(bf16[128,32,128]{2,1,0:T(8,128)(2,1)} %fusion.17) | data formatting | bytes 2097152 | tf_op jit(solution)/shard_map/convert_element_type | solution.py:92
  64.6 2.6 %copy.82 = bf16[128,8,512]{2,0,1:T(8,128)(2,1)} copy(bf16[128,8,512]{2,1,0:T(8,128)(2,1)} %convert_element_type.97) | data formatting | bytes 2097152 | tf_op jit(solution)/shard_map/convert_element_type | solution.py:92
  67.2 4.2 %all-to-all-start.1 = ((bf16[128,8,512]{2,0,1:T(8,128)(2,1)}), bf16[128,8,512]{2,0,1:T(8,128)(2,1)}, u32[]{:S(2)}, u32[]{:S(2)}) async-start(bf16[128,8,512]{2,0,1:T(8,128)(2,1)} %copy.82), calls=%async_computation.1 | async-start | bytes 2097152 | tf_op jit(solution)/shard_map/all_to_all | solution.py:60
  71.5 2.9 %multiply_convert_fusion = bf16[32,128,128]{2,1,0:T(8,128)(2,1)} fusion(f32[32]{0:T(128)S(1)} %fusion.83, bf16[32,128,128]{2,1,0:T(8,128)(2,1)} %gather_fusion.2, pred[32]{0:T(512)(128)(4,1)S(1)} %get-tuple-element.27, bf16[32,128,128]{2,1,0:T(8,128)(2,1)S(1)} %copy-done.11, pred[32]{0:T(512)(128)(4,1)S(1)} %get-tuple-element.11), kind=kOutput, calls=%fused_computation.20 | convolution fusion | flops 136314880 | bytes 3145920 | tf_op jit(solution)/shard_map/tsk,tsn->skn/dot_general | solution.py:38
  74.4 1.7 gather_fusion.4
  76.1 1.8 gather_fusion.5
  77.9 2.0 %multiply_convert_fusion.2 = bf16[32,128,128]{2,1,0:T(8,128)(2,1)S(1)} fusion(f32[32]{0:T(128)S(1)} %fusion.84, bf16[32,128,128]{2,1,0:T(8,128)(2,1)S(1)} %copy-done.9, pred[32]{0:T(512)(128)(4,1)S(1)} %get-tuple-element.29, bf16[32,128,128]{2,1,0:T(8,128)(2,1)} %gather_fusion.4, pred[32]{0:T(512)(128)(4,1)S(1)} %get-tuple-element.7), kind=kOutput, calls=%fused_computation.22 | convolution fusion | flops 136314880 | bytes 3145920 | tf_op jit(solution)/shard_map/tsk,tsn->skn/dot_general | solution.py:38
  80.0 0.7 multiply_convert_fusion.1
  80.7 0.5 copy-done.14
  81.2 0.3 pad_maximum_fusion
  81.5 2.0 %copy.100 = bf16[8,4,3,128,128]{4,3,0,2,1:T(8,128)(2,1)} copy(bf16[8,4,3,128,128]{4,3,1,0,2:T(8,128)(2,1)S(1)} %pad_maximum_fusion) | data formatting | bytes 6291456 | tf_op jit(solution)/shard_map/stack | solution.py:113
  83.6 3.8 %all-to-all-done.1 = bf16[128,8,512]{2,0,1:T(8,128)(2,1)} async-done(((bf16[128,8,512]{2,0,1:T(8,128)(2,1)}), bf16[128,8,512]{2,0,1:T(8,128)(2,1)}, u32[]{:S(2)}, u32[]{:S(2)}) %all-to-all-start.1) | async-done | bytes 1048608 | tf_op jit(solution)/shard_map/all_to_all | solution.py:60
  87.4 6.0 %all-to-all-start.3 = ((bf16[8,4,3,128,128]{4,3,0,2,1:T(8,128)(2,1)}), bf16[8,4,3,128,128]{4,3,0,2,1:T(8,128)(2,1)}, u32[]{:S(2)}, u32[]{:S(2)}) async-start(bf16[8,4,3,128,128]{4,3,0,2,1:T(8,128)(2,1)} %copy.100), calls=%async_computation.3 | async-start | bytes 6291456 | tf_op jit(solution)/shard_map/all_to_all | solution.py:53
  93.4 2.6 %convolution_bitcast_fusion = f32[128,32,128]{2,0,1:T(8,128)S(1)} fusion(bf16[1,32,128,128]{3,2,1,0:T(8,128)(2,1)} %param.17, bf16[32,128,128]{2,1,0:T(8,128)(2,1)} %gather_fusion.5, pred[32]{0:T(512)(128)(4,1)S(1)} %get-tuple-element.9), kind=kOutput, calls=%fused_computation.24 | convolution fusion | flops 134742016 | bytes 4194336 | tf_op jit(solution)/shard_map/tsn,skn->tsk/dot_general | solution.py:34
  96.0 0.9 convolution_bitcast_fusion.1
  96.9 3.0 %fusion = f32[32,128,128]{2,0,1:T(8,128)S(1)} fusion(f32[128,32,128]{2,0,1:T(8,128)S(1)} %convolution_bitcast_fusion, f32[32]{0:T(128)S(1)} %fusion.85, s32[32]{0:T(128)S(1)} %get-tuple-element.32), kind=kOutput, calls=%fused_computation.7 | convolution fusion | flops 201328640 | bytes 4194560 | tf_op jit(solution)/shard_map/tsn,sc->tcn/dot_general | solution.py:22
  99.9 3.1 %fusion.20 = bf16[128,32,128]{2,1,0:T(8,128)(2,1)S(1)} fusion(f32[32,128,128]{2,0,1:T(8,128)S(1)} %fusion, f32[128,32,128]{2,0,1:T(8,128)S(1)} %convolution_bitcast_fusion.1, f32[32]{0:T(128)S(1)} %fusion.84, s32[32]{0:T(128)S(1)} %get-tuple-element.30), kind=kOutput, calls=%fused_computation.33 | convolution fusion | flops 202377216 | bytes 5243136 | tf_op jit(solution)/shard_map/tsn,sc->tcn/dot_general | solution.py:22
  103.0 0.7 convert_element_type.102
  103.7 1.4 copy.88
  105.1 24.5 %all-to-all-done.3 = bf16[8,4,3,128,128]{4,3,0,2,1:T(8,128)(2,1)} async-done(((bf16[8,4,3,128,128]{4,3,0,2,1:T(8,128)(2,1)}), bf16[8,4,3,128,128]{4,3,0,2,1:T(8,128)(2,1)}, u32[]{:S(2)}, u32[]{:S(2)}) %all-to-all-start.3) | async-done | bytes 3145760 | tf_op jit(solution)/shard_map/all_to_all | solution.py:53
  129.6 3.6 %all-to-all-start.2 = ((bf16[128,8,512]{2,0,1:T(8,128)(2,1)}), bf16[128,8,512]{2,0,1:T(8,128)(2,1)S(1)}, u32[]{:S(2)}, u32[]{:S(2)}) async-start(bf16[128,8,512]{2,0,1:T(8,128)(2,1)} %copy.88), calls=%async_computation.2 | async-start | bytes 2097152 | tf_op jit(solution)/shard_map/all_to_all | solution.py:60
  133.1 2.6 %reduce_sum.47 = bf16[8,3,128,128]{3,2,0,1:T(8,128)(2,1)S(1)} reduce(bf16[8,4,3,128,128]{4,3,0,2,1:T(8,128)(2,1)} %all-to-all-done.3, bf16[]{:T(256)} %constant.110.clone.1), dimensions={1}, to_apply=%region_2.5 | reduce | flops 1179648 | bytes 3932162 | tf_op jit(solution)/shard_map/reduce_sum | solution.py:53
  135.7 1.0 copy.96
  136.7 12.3 %all-to-all-done.2 = bf16[128,8,512]{2,0,1:T(8,128)(2,1)S(1)} async-done(((bf16[128,8,512]{2,0,1:T(8,128)(2,1)}), bf16[128,8,512]{2,0,1:T(8,128)(2,1)S(1)}, u32[]{:S(2)}, u32[]{:S(2)}) %all-to-all-start.2) | async-done | bytes 1048608 | tf_op jit(solution)/shard_map/all_to_all | solution.py:60
  149.0 7.6 %all-to-all-start.4 = ((bf16[8,3,128,128]{3,2,1,0:T(8,128)(2,1)}), bf16[8,3,128,128]{3,2,1,0:T(8,128)(2,1)S(1)}, u32[]{:S(2)}, u32[]{:S(2)}) async-start(bf16[8,3,128,128]{3,2,1,0:T(8,128)(2,1)} %copy.96), calls=%async_computation.4 | async-start | bytes 1572864 | tf_op jit(solution)/shard_map/all_to_all | solution.py:54
  156.6 2.1 %reduce_sum.45 = bf16[128,512]{1,0:T(8,128)(2,1)} reduce(bf16[128,8,512]{2,0,1:T(8,128)(2,1)} %all-to-all-done.1, bf16[]{:T(256)} %constant.110.clone.1), dimensions={1}, to_apply=%region_0.3 | reduce | flops 458752 | bytes 1179650 | tf_op jit(solution)/shard_map/reduce_sum | solution.py:61
  158.6 0.8 reduce_sum.46
  159.5 19.9 %all-to-all-done.4 = bf16[8,3,128,128]{3,2,1,0:T(8,128)(2,1)S(1)} async-done(((bf16[8,3,128,128]{3,2,1,0:T(8,128)(2,1)}), bf16[8,3,128,128]{3,2,1,0:T(8,128)(2,1)S(1)}, u32[]{:S(2)}, u32[]{:S(2)}) %all-to-all-start.4) | async-done | bytes 786464 | tf_op jit(solution)/shard_map/all_to_all | solution.py:54
  179.5 0.7 fusion.105
  (54 shorter events, 0.7 us)
Async XLA Ops:
  0.6 48.8 %copy-start = (bf16[1,32,128,128]{3,2,1,0:T(8,128)(2,1)S(1)}, bf16[1,32,128,128]{3,2,1,0:T(8,128)(2,1)}, u32[]{:S(2)}) copy-start(bf16[1,32,128,128]{3,2,1,0:T(8,128)(2,1)} %param.19) | copy-start | bytes 3145732
  3.7 4.4 %copy-start.16 = (s32[1,32]{1,0:T(1,128)S(1)}, s32[1,32]{1,0:T(1,128)}, u32[]{:S(2)}) copy-start(s32[1,32]{1,0:T(1,128)} %param.16) | copy-start | bytes 388
  3.7 4.5 %copy-start.17 = (s32[1,32]{1,0:T(1,128)S(1)}, s32[1,32]{1,0:T(1,128)}, u32[]{:S(2)}) copy-start(s32[1,32]{1,0:T(1,128)} %param.18) | copy-start | bytes 388
  3.7 4.6 %copy-start.15 = (s32[1,32]{1,0:T(1,128)S(1)}, s32[1,32]{1,0:T(1,128)}, u32[]{:S(2)}) copy-start(s32[1,32]{1,0:T(1,128)} %param.14) | copy-start | bytes 388
  3.7 31.6 %all-to-all-start = ((bf16[8,2,128,512]{2,3,1,0:T(8,128)(2,1)}), bf16[8,2,128,512]{2,3,1,0:T(8,128)(2,1)S(1)}, u32[]{:S(2)}, u32[]{:S(2)}) async-start(bf16[8,2,128,512]{2,3,1,0:T(8,128)(2,1)} %broadcast_in_dim.22), calls=%async_computation | async-start | bytes 4194304 | tf_op jit(solution)/shard_map/all_to_all | solution.py:45
  39.2 4.6 %copy-start.4 = (bf16[1,32,128,128]{3,2,1,0:T(8,128)(2,1)S(1)}, bf16[1,32,128,128]{3,2,1,0:T(8,128)(2,1)}, u32[]{:S(2)}) copy-start(bf16[1,32,128,128]{3,2,1,0:T(8,128)(2,1)} %param.15) | copy-start | bytes 3145732
  40.9 3.0 %copy-start.8 = (bf16[32,128,128]{2,1,0:T(8,128)(2,1)S(1)}, bf16[32,128,128]{2,1,0:T(8,128)(2,1)}, u32[]{:S(2)}) copy-start(bf16[32,128,128]{2,1,0:T(8,128)(2,1)} %gather_fusion) | copy-start | bytes 3145732
  44.3 2.3 %copy-start.3 = (bf16[1,32,128,128]{3,2,1,0:T(8,128)(2,1)S(1)}, bf16[1,32,128,128]{3,2,1,0:T(8,128)(2,1)}, u32[]{:S(2)}) copy-start(bf16[1,32,128,128]{3,2,1,0:T(8,128)(2,1)} %param.17) | copy-start | bytes 3145732
  44.4 2.3 %copy-start.6 = (bf16[32,128,128]{2,1,0:T(8,128)(2,1)S(1)}, bf16[32,128,128]{2,1,0:T(8,128)(2,1)}, u32[]{:S(2)}) copy-start(bf16[32,128,128]{2,1,0:T(8,128)(2,1)} %gather_fusion.1) | copy-start | bytes 3145732
  47.1 2.3 %copy-start.10 = (bf16[32,128,128]{2,1,0:T(8,128)(2,1)S(1)}, bf16[32,128,128]{2,1,0:T(8,128)(2,1)}, u32[]{:S(2)}) copy-start(bf16[32,128,128]{2,1,0:T(8,128)(2,1)} %gather_fusion.3) | copy-start | bytes 3145732
  64.6 6.8 %copy-start.11 = (bf16[32,128,128]{2,1,0:T(8,128)(2,1)S(1)}, bf16[32,128,128]{2,1,0:T(8,128)(2,1)}, u32[]{:S(2)}) copy-start(bf16[32,128,128]{2,1,0:T(8,128)(2,1)} %gather_fusion.3) | copy-start | bytes 3145732
  67.2 20.2 %all-to-all-start.1 = ((bf16[128,8,512]{2,0,1:T(8,128)(2,1)}), bf16[128,8,512]{2,0,1:T(8,128)(2,1)}, u32[]{:S(2)}, u32[]{:S(2)}) async-start(bf16[128,8,512]{2,0,1:T(8,128)(2,1)} %copy.82), calls=%async_computation.1 | async-start | bytes 2097152 | tf_op jit(solution)/shard_map/all_to_all | solution.py:60
  71.4 2.9 %copy-start.2 = (bf16[128,14,128]{2,0,1:T(8,128)(2,1)S(1)}, bf16[128,14,128]{2,0,1:T(8,128)(2,1)}, u32[]{:S(2)}) copy-start(bf16[128,14,128]{2,0,1:T(8,128)(2,1)} %get-tuple-element.19) | copy-start | bytes 1376260
  74.4 1.8 copy-start.1
  74.4 3.5 %copy-start.9 = (bf16[32,128,128]{2,1,0:T(8,128)(2,1)S(1)}, bf16[32,128,128]{2,1,0:T(8,128)(2,1)}, u32[]{:S(2)}) copy-start(bf16[32,128,128]{2,1,0:T(8,128)(2,1)} %gather_fusion) | copy-start | bytes 3145732
  77.9 2.1 %copy-start.7 = (bf16[32,128,128]{2,1,0:T(8,128)(2,1)S(1)}, bf16[32,128,128]{2,1,0:T(8,128)(2,1)}, u32[]{:S(2)}) copy-start(bf16[32,128,128]{2,1,0:T(8,128)(2,1)} %gather_fusion.1) | copy-start | bytes 3145732
  77.9 2.1 %copy-start.13 = (bf16[32,128,128]{2,1,0:T(8,128)(2,1)S(1)}, bf16[32,128,128]{2,1,0:T(8,128)(2,1)}, u32[]{:S(2)}) copy-start(bf16[32,128,128]{2,1,0:T(8,128)(2,1)} %gather_fusion.5) | copy-start | bytes 3145732
  80.0 1.2 copy-start.14
  87.4 42.2 %all-to-all-start.3 = ((bf16[8,4,3,128,128]{4,3,0,2,1:T(8,128)(2,1)}), bf16[8,4,3,128,128]{4,3,0,2,1:T(8,128)(2,1)}, u32[]{:S(2)}, u32[]{:S(2)}) async-start(bf16[8,4,3,128,128]{4,3,0,2,1:T(8,128)(2,1)} %copy.100), calls=%async_computation.3 | async-start | bytes 6291456 | tf_op jit(solution)/shard_map/all_to_all | solution.py:53
  93.4 2.6 %copy-start.5 = (bf16[1,32,128,128]{3,2,1,0:T(8,128)(2,1)S(1)}, bf16[1,32,128,128]{3,2,1,0:T(8,128)(2,1)}, u32[]{:S(2)}) copy-start(bf16[1,32,128,128]{3,2,1,0:T(8,128)(2,1)} %param.15) | copy-start | bytes 3145732
  93.4 2.6 %copy-start.12 = (bf16[32,128,128]{2,1,0:T(8,128)(2,1)S(1)}, bf16[32,128,128]{2,1,0:T(8,128)(2,1)}, u32[]{:S(2)}) copy-start(bf16[32,128,128]{2,1,0:T(8,128)(2,1)} %gather_fusion.4) | copy-start | bytes 3145732
  129.6 19.4 %all-to-all-start.2 = ((bf16[128,8,512]{2,0,1:T(8,128)(2,1)}), bf16[128,8,512]{2,0,1:T(8,128)(2,1)S(1)}, u32[]{:S(2)}, u32[]{:S(2)}) async-start(bf16[128,8,512]{2,0,1:T(8,128)(2,1)} %copy.88), calls=%async_computation.2 | async-start | bytes 2097152 | tf_op jit(solution)/shard_map/all_to_all | solution.py:60
  149.0 30.4 %all-to-all-start.4 = ((bf16[8,3,128,128]{3,2,1,0:T(8,128)(2,1)}), bf16[8,3,128,128]{3,2,1,0:T(8,128)(2,1)S(1)}, u32[]{:S(2)}, u32[]{:S(2)}) async-start(bf16[8,3,128,128]{3,2,1,0:T(8,128)(2,1)} %copy.96), calls=%async_computation.4 | async-start | bytes 1572864 | tf_op jit(solution)/shard_map/all_to_all | solution.py:54
